TPU v7x, 512 devices: a whole 4x8x8 slice. The times are simulated.
512 devices in a mesh: space: 32 (over x, y_hi, core), tm: 16 (over z, y_lo).
Axes of the slice: x: 4, y: 8 (y_hi: 4, y_lo: 2; y = y_hi * 2 + y_lo), z: 8, core: 2. Of those that a mesh axis runs over, the one named last changes fastest.
Arguments:
- field: float32 [256, 32768], P('tm', 'space'), may hold values from -6 to 6
- momentum: float32 [256, 32768], P('tm', 'space'), may hold values from -6 to 6
- solution: float32 [256, 32768], P('tm', 'space'), may hold values from -6 to 6
- tiles: float32 [256, 6, 128, 128], P('space'), may hold values from -1 to 2
- columns: int32 [256, 6], P('space'), may hold values from 0 to 255, as said below
- neighbours: int32 [3, 32768], P(None, 'space'), may hold values from 0 to 32767, as said below
Outputs:
- field_out: float32 [256, 32768], P('tm', 'space')
- momentum_out: float32 [256, 32768], P('tm', 'space')
- fermion_force: float32 [256, 32768], P('tm', 'space')
Inputs may be any that keep to these rules, and one draw needn't show every extreme that they name: Row r lists 6 different tile columns, the first of them r itself; the others lie outside the run of 8 tile rows that holds r (runs r // 8), and the rows of one run name at most 2 columns of any other run, exactly 2 for some run. The neighbour relation is symmetric, each site has three different neighbours, and each neighbour lies in the site's own run of 128 labels or in the run just before or after it, cyclically over the flake.
All inputs are finite; a program needn't handle non-finite values.
Results may differ from a plain program's by a relative error of at most 0.00014.
Values sent between devices are 32-bit elements; how exact they have to be, the bound alone decides.
No kernel may reach another device: no remote copies, remote signals or barrier semaphores. Data moves between devices by JAX's collectives and lax.ppermute only.
A program may use at most 64 MiB of HBM per device.

v0:
```python
import jax
import jax.numpy as jnp
from jax import lax
from jax.sharding import PartitionSpec as P

TILE = 128
step_size = 0.5
hop_kappa = 0.5
coupling = 0.25


def with_halo(block, sides, width):
    for axis, dim in sides:
        count = lax.axis_size(axis)
        forward = [(i, i + 1) for i in range(count - 1)]
        forward.append((count - 1, 0))
        backward = [(target, source) for source, target in forward]
        low = lax.ppermute(
            lax.slice_in_dim(block, block.shape[dim] - width, None, axis=dim), axis, forward
        )
        high = lax.ppermute(lax.slice_in_dim(block, 0, width, axis=dim), axis, backward)
        block = jnp.concatenate([low, block, high], axis=dim)
    return block


def from_behind(value, axis, steps):
    count = lax.axis_size(axis)
    pairs = [(source, (source + steps) % count) for source in range(count)]
    return lax.ppermute(value, axis, pairs)


def body(field, momentum, solution, tiles, columns, neighbours):
    slices = field.shape[0]
    tile_rows = tiles.shape[0]
    kept = tiles.shape[1]
    site_count = field.shape[1]
    cols_flat = columns.reshape(-1)
    space_count = lax.axis_size("space")

    def coulomb(values):
        gathered = lax.all_gather(values, "space", axis=1, tiled=True)
        blocks = gathered.reshape(slices, -1, TILE)
        picked = jnp.take(blocks, cols_flat, axis=1).reshape(slices, tile_rows, kept, TILE)
        mixed = jnp.einsum("rkij,trkj->tri", tiles, picked, precision=lax.Precision.HIGHEST)
        return mixed.reshape(slices, site_count)

    moment = momentum - 0.5 * step_size * coulomb(field)
    field_one = field + step_size * moment
    moment = moment - step_size * coulomb(field_one)
    field_two = field_one + step_size * moment
    moment = moment - 0.5 * step_size * coulomb(field_two)
    total_sites = site_count * space_count
    first_site = lax.axis_index("space") * site_count
    lookup = (neighbours - first_site + TILE) % total_sites
    parity_sign = jnp.where(lax.axis_index("tm") == 0, -1.0, 1.0).astype(jnp.float32)
    widened = with_halo(solution, (("space", 1),), TILE)
    beside = jnp.take(widened, lookup.reshape(-1), axis=1).reshape(solution.shape[0], 3, site_count)
    hopped = solution + hop_kappa * (beside[:, 0] + beside[:, 1] + beside[:, 2])
    arrived = from_behind(hopped[-1:], "tm", 1)
    earlier = jnp.concatenate([parity_sign * arrived, hopped[:-1]], axis=0)
    link_factor = jnp.exp(coupling * field_two)
    shifted = solution - link_factor * earlier
    force = 2.0 * coupling * shifted * link_factor * earlier
    return (field_two, moment, force)


def solution(mesh):
    in_specs = (
        P("tm", "space"),
        P("tm", "space"),
        P("tm", "space"),
        P("space", None, None, None),
        P("space", None),
        P(None, "space"),
    )
    out_specs = (P("tm", "space"), P("tm", "space"), P("tm", "space"))
    return jax.shard_map(body, mesh=mesh, in_specs=in_specs, out_specs=out_specs, check_vma=False)
```

profile of v0, /device:TPU:1, one launch (start us, length us, event | category | flops | bytes accessed | tf_op | source)
XLA Modules:
  0.0 224.8 jit_solution(11539361856187728963)
XLA Ops:
  7.2 0.0 copy-start
  7.2 0.0 all-gather.4.cloned.1.call-start
  7.2 0.7 all-gather.4.cloned.1.call-update
  7.9 0.0 all-gather.6.cloned.1.call-start
  8.0 0.9 reshape.89
  8.9 67.8 %all-gather.4.cloned.1.call-done = f32[16,32768]{1,0:T(8,128)} async-done(((f32[16,1024]{1,0:T(8,128)}), f32[16,32768]{1,0:T(8,128)}) %all-gather.4.cloned.1.call-update) | async-done | bytes 2097168 | tf_op jit(solution)/shard_map/all_gather | solution.py:41
  76.7 3.1 %copy_bitcast_fusion.2 = f32[16,256,128]{2,0,1:T(8,128)} fusion(f32[16,32768]{1,0:T(8,128)} %all-gather.4.cloned.1.call-done), kind=kLoop, calls=%fused_computation.6 | loop fusion | bytes 4194304 | tf_op jit(solution)/shard_map/reshape | solution.py:42
  79.8 2.2 gather_fusion.1
  82.0 0.0 copy-start.8
  82.0 0.0 copy-start.14
  82.0 0.1 broadcast_select_fusion.2
  82.1 0.0 copy-start.4
  82.1 0.0 copy-start.15
  82.2 2.7 %fusion.5 = f32[8,2,8,128]{3,2,1,0:T(8,128)S(1)} fusion(f32[16,8,6,128]{3,0,2,1:T(8,128)S(1)} %bitcast.95, f32[8,6,128,128]{3,2,1,0:T(8,128)S(1)} %copy-done), kind=kOutput, calls=%fused_computation.15 | convolution fusion | flops 151011328 | bytes 3604480 | tf_op jit(solution)/shard_map/rkij,trkj->tri/dot_general | solution.py:44
  84.9 0.6 copy-done.1
  85.5 0.6 multiply_add_fusion.1
  86.2 0.0 all-gather.6.cloned.1.call-update
  86.2 0.0 all-gather.8.cloned.1.call-start
  86.3 3.0 %collective-permute-start = (f32[16,128]{1,0:T(8,128)S(1)}, f32[16,128]{1,0:T(8,128)S(1)}, u32[]{:S(2)}, u32[]{:S(2)}) collective-permute-start(f32[16,128]{1,0:T(8,128)S(1)} %get-tuple-element.8), channel_id=1, source_target_pairs={{0,16},{16,32},{32,48},{48,64},{64,80},{80,96},{96,112},{112,128},... | collective-permute-start | bytes 24584 | tf_op jit(solution)/shard_map/ppermute | solution.py:18
  89.3 1.9 collective-permute-start.1
  91.3 4.0 %collective-permute-done.1 = f32[16,128]{1,0:T(8,128)S(1)} collective-permute-done((f32[16,128]{1,0:T(8,128)S(1)}, f32[16,128]{1,0:T(8,128)S(1)}, u32[]{:S(2)}, u32[]{:S(2)}) %collective-permute-start.1) | collective-permute-done | bytes 8224 | tf_op jit(solution)/shard_map/ppermute | solution.py:21
  95.3 1.1 copy.39
  96.4 12.0 %gather_fusion = f32[3072,16]{1,0:T(8,128)} fusion(f32[16,1280]{0,1:T(8,128)} %copy.39, s32[3072]{0:T(1024)S(1)} %broadcast_clamp_fusion), kind=kCustom, calls=%fused_computation.3 | custom fusion | bytes 405504 | tf_op jit(solution)/shard_map/jit(_take)/gather | solution.py:57
  108.4 1.8 copy.40
  110.3 0.0 copy-start.12
  110.3 0.6 copy-done.12
  110.9 2.7 %collective-permute-start.2 = (f32[1,1024]{1,0:T(1,128)S(1)}, f32[1,1024]{1,0:T(1,128)S(1)}, u32[]{:S(2)}, u32[]{:S(2)}) collective-permute-start(f32[1,1024]{1,0:T(1,128)S(1)} %slice.39), channel_id=1, source_target_pairs={{0,1},{1,2},{2,3},{3,4},{4,5},{5,6},{6,7},{7,8},{8,9},{9,10},{10,1... | collective-permute-start | bytes 12296 | tf_op jit(solution)/shard_map/ppermute | solution.py:29
  113.6 4.4 %collective-permute-done.2 = f32[1,1024]{1,0:T(1,128)S(1)} collective-permute-done((f32[1,1024]{1,0:T(1,128)S(1)}, f32[1,1024]{1,0:T(1,128)S(1)}, u32[]{:S(2)}, u32[]{:S(2)}) %collective-permute-start.2) | collective-permute-done | bytes 4128 | tf_op jit(solution)/shard_map/ppermute | solution.py:29
  118.0 25.4 %all-gather.6.cloned.1.call-done = f32[16,32768]{1,0:T(8,128)} async-done(((f32[16,1024]{1,0:T(8,128)}), f32[16,32768]{1,0:T(8,128)}) %all-gather.6.cloned.1.call-update) | async-done | bytes 2097168 | tf_op jit(solution)/shard_map/all_gather | solution.py:41
  143.4 3.1 %copy_bitcast_fusion.1 = f32[16,256,128]{2,0,1:T(8,128)} fusion(f32[16,32768]{1,0:T(8,128)} %all-gather.6.cloned.1.call-done), kind=kLoop, calls=%fused_computation.5 | loop fusion | bytes 4194304 | tf_op jit(solution)/shard_map/reshape | solution.py:42
  146.5 2.2 gather_fusion.2
  148.6 0.0 copy-start.5
  148.7 0.0 copy-start.9
  148.7 0.0 copy-start.11
  148.7 0.0 copy-start.13
  148.7 0.1 broadcast_select_fusion.1
  148.8 2.7 %fusion.3 = f32[8,2,8,128]{3,2,1,0:T(8,128)S(1)} fusion(f32[16,8,6,128]{3,0,2,1:T(8,128)S(1)} %bitcast.96, f32[8,6,128,128]{3,2,1,0:T(8,128)S(1)} %copy-done), kind=kOutput, calls=%fused_computation.12 | convolution fusion | flops 151011328 | bytes 3604480 | tf_op jit(solution)/shard_map/rkij,trkj->tri/dot_general | solution.py:44
  151.5 0.0 copy-done.2
  151.6 0.7 multiply_multiply_fusion
  152.3 0.0 all-gather.8.cloned.1.call-update
  152.3 57.2 %all-gather.8.cloned.1.call-done = f32[16,32768]{1,0:T(8,128)} async-done(((f32[16,1024]{1,0:T(8,128)}), f32[16,32768]{1,0:T(8,128)}) %all-gather.8.cloned.1.call-update) | async-done | bytes 2097168 | tf_op jit(solution)/shard_map/all_gather | solution.py:41
  209.5 3.1 %copy_bitcast_fusion = f32[16,256,128]{2,0,1:T(8,128)} fusion(f32[16,32768]{1,0:T(8,128)} %all-gather.8.cloned.1.call-done), kind=kLoop, calls=%fused_computation.4 | loop fusion | bytes 4194304 | tf_op jit(solution)/shard_map/reshape | solution.py:42
  212.6 2.2 gather_fusion.3
  214.8 0.0 copy-start.10
  214.8 0.1 broadcast_select_fusion
  214.9 2.7 %fusion.1 = f32[8,2,8,128]{3,2,1,0:T(8,128)S(1)} fusion(f32[16,8,6,128]{3,0,2,1:T(8,128)S(1)} %bitcast.94, f32[8,6,128,128]{3,2,1,0:T(8,128)S(1)} %copy-done), kind=kOutput, calls=%fused_computation.9 | convolution fusion | flops 151011328 | bytes 3604480 | tf_op jit(solution)/shard_map/rkij,trkj->tri/dot_general | solution.py:44
  217.6 0.0 copy-done.7
  217.7 0.6 bitcast_subtract_fusion
  (31 shorter events, 0.2 us)
Async XLA Ops:
  7.2 75.0 %copy-start = (f32[8,6,128,128]{3,2,1,0:T(8,128)S(1)}, f32[8,6,128,128]{3,2,1,0:T(8,128)}, u32[]{:S(2)}) copy-start(f32[8,6,128,128]{3,2,1,0:T(8,128)} %param.11) | copy-start | bytes 9437188
  7.2 69.6 %all-gather.4.cloned.1.call-start = ((), (), s32[]{:S(2)}) async-start(), calls=%async_computation | async-start | bytes 2162688 | tf_op jit(solution)/shard_map/all_gather | solution.py:41
  7.9 135.5 %all-gather.6.cloned.1.call-start = ((), (), s32[]{:S(2)}) async-start(), calls=%async_computation.1 | async-start | bytes 2162688 | tf_op jit(solution)/shard_map/all_gather | solution.py:41
  82.0 3.6 %copy-start.8 = (f32[16,1024]{1,0:T(8,128)S(1)}, f32[16,1024]{1,0:T(8,128)}, u32[]{:S(2)}) copy-start(f32[16,1024]{1,0:T(8,128)} %param.9) | copy-start | bytes 196612
  82.0 3.6 %copy-start.14 = (f32[16,1024]{1,0:T(8,128)S(1)}, f32[16,1024]{1,0:T(8,128)}, u32[]{:S(2)}) copy-start(f32[16,1024]{1,0:T(8,128)} %param.8) | copy-start | bytes 196612
  82.1 4.1 %copy-start.4 = (f32[16,1024]{1,0:T(8,128)S(1)}, f32[16,1024]{1,0:T(8,128)}, u32[]{:S(2)}) copy-start(f32[16,1024]{1,0:T(8,128)} %param.10) | copy-start | bytes 196612
  82.1 9.1 %copy-start.15 = (s32[3,1024]{1,0:T(4,128)S(1)}, s32[3,1024]{1,0:T(4,128)}, u32[]{:S(2)}) copy-start(s32[3,1024]{1,0:T(4,128)} %param.13) | copy-start | bytes 36868
  84.9 0.6 copy-start.1
  86.2 123.3 %all-gather.8.cloned.1.call-start = ((), (), s32[]{:S(2)}) async-start(), calls=%async_computation.2 | async-start | bytes 2162688 | tf_op jit(solution)/shard_map/all_gather | solution.py:41
  86.3 5.0 %collective-permute-start = (f32[16,128]{1,0:T(8,128)S(1)}, f32[16,128]{1,0:T(8,128)S(1)}, u32[]{:S(2)}, u32[]{:S(2)}) collective-permute-start(f32[16,128]{1,0:T(8,128)S(1)} %get-tuple-element.8), channel_id=1, source_target_pairs={{0,16},{16,32},{32,48},{48,64},{64,80},{80,96},{96,112},{112,128},... | collective-permute-start | bytes 24584 | tf_op jit(solution)/shard_map/ppermute | solution.py:18
  89.3 6.1 %collective-permute-start.1 = (f32[16,128]{1,0:T(8,128)S(1)}, f32[16,128]{1,0:T(8,128)S(1)}, u32[]{:S(2)}, u32[]{:S(2)}) collective-permute-start(f32[16,128]{1,0:T(8,128)S(1)} %get-tuple-element.9), channel_id=1, source_target_pairs={{16,0},{32,16},{48,32},{64,48},{80,64},{96,80},{112,96},{128,112},... | collective-permute-start | bytes 24584 | tf_op jit(solution)/shard_map/ppermute | solution.py:21
  110.3 0.6 copy-start.12
  110.9 7.0 %collective-permute-start.2 = (f32[1,1024]{1,0:T(1,128)S(1)}, f32[1,1024]{1,0:T(1,128)S(1)}, u32[]{:S(2)}, u32[]{:S(2)}) collective-permute-start(f32[1,1024]{1,0:T(1,128)S(1)} %slice.39), channel_id=1, source_target_pairs={{0,1},{1,2},{2,3},{3,4},{4,5},{5,6},{6,7},{7,8},{8,9},{9,10},{10,1... | collective-permute-start | bytes 12296 | tf_op jit(solution)/shard_map/ppermute | solution.py:29
  148.6 2.9 %copy-start.2 = (f32[8,2,8,128]{3,2,1,0:T(8,128)S(1)}, f32[8,2,8,128]{3,2,1,0:T(8,128)}, u32[]{:S(2)}) copy-start(f32[8,2,8,128]{3,2,1,0:T(8,128)} %copy-done.1) | copy-start | bytes 196612
  148.6 2.9 %copy-start.5 = (f32[16,1024]{1,0:T(8,128)S(1)}, f32[16,1024]{1,0:T(8,128)}, u32[]{:S(2)}) copy-start(f32[16,1024]{1,0:T(8,128)} %param.10) | copy-start | bytes 196612
  148.7 2.9 %copy-start.9 = (f32[16,1024]{1,0:T(8,128)S(1)}, f32[16,1024]{1,0:T(8,128)}, u32[]{:S(2)}) copy-start(f32[16,1024]{1,0:T(8,128)} %param.9) | copy-start | bytes 196612
  148.7 2.9 %copy-start.11 = (f32[16,1024]{1,0:T(8,128)S(1)}, f32[16,1024]{1,0:T(8,128)}, u32[]{:S(2)}) copy-start(f32[16,1024]{1,0:T(8,128)} %multiply_add_fusion.1) | copy-start | bytes 196612
  148.7 2.9 %copy-start.13 = (f32[16,1024]{1,0:T(8,128)S(1)}, f32[16,1024]{1,0:T(8,128)}, u32[]{:S(2)}) copy-start(f32[16,1024]{1,0:T(8,128)} %copy-done.12) | copy-start | bytes 196612
  151.5 0.8 copy-start.6
  214.7 2.9 %copy-start.3 = (f32[8,2,8,128]{3,2,1,0:T(8,128)S(1)}, f32[8,2,8,128]{3,2,1,0:T(8,128)}, u32[]{:S(2)}) copy-start(f32[8,2,8,128]{3,2,1,0:T(8,128)} %copy-done.1) | copy-start | bytes 196612
  214.8 2.9 %copy-start.7 = (f32[8,2,8,128]{3,2,1,0:T(8,128)S(1)}, f32[8,2,8,128]{3,2,1,0:T(8,128)}, u32[]{:S(2)}) copy-start(f32[8,2,8,128]{3,2,1,0:T(8,128)} %copy-done.6) | copy-start | bytes 196612
  214.8 2.9 %copy-start.10 = (f32[16,1024]{1,0:T(8,128)S(1)}, f32[16,1024]{1,0:T(8,128)}, u32[]{:S(2)}) copy-start(f32[16,1024]{1,0:T(8,128)} %param.9) | copy-start | bytes 196612
Sparse Core Ops, SparseCore 0:
  11.2 65.4 all-gather.3
  86.3 57.0 all-gather.5
  152.5 57.0 all-gather.7
where the time goes:
time: 225 us
  waiting for transfers between devices  160 us (71%)
  local copies, waits for them, and re-layouts  32.9 us (15%)
  between operations  14.1 us (6%)
  matrix products  8.19 us (4%)
  starting transfers between devices  7.67 us (3%)
  other arithmetic  2.47 us (1%)
    all_gather x3, waiting for transfers between devices, coulomb(): gathered = lax.all_gather(values, 'space', axis=1, tiled=True)  150 us
    gather x2, local copies, waits for them, and re-layouts, body(): jnp.take(widened, lookup.reshape(-1), axis=1)  13.8 us
    reshape x3, local copies, waits for them, and re-layouts, coulomb(): blocks = gathered.reshape(slices, -1, TILE)  9.16 us
    dot_general x3, matrix products, coulomb(): jnp.einsum('rkij,trkj->tri', tiles, picked, precision=lax.Precision.HIGHEST)  8.19 us
    gather x3, local copies, waits for them, and re-layouts, coulomb(): jnp.take(blocks, cols_flat, axis=1).reshape(slices, tile_rows, kept, TILE)  6.51 us
  transfers between devices with their start and end apart: 6, of which 5 were waited for; matrix products, arithmetic and copies ran while one was open for 7% of the time, Pallas kernels for 0%

commit v1 on v0

--- a/solution.py
+++ b/solution.py
@@ -38,7 +38,9 @@
     space_count = lax.axis_size("space")
 
     def coulomb(values):
-        gathered = lax.all_gather(values, "space", axis=1, tiled=True)
+        gathered = jnp.concatenate(
+            lax.all_to_all(jnp.stack([values] * lax.axis_size("space")), "space", 0, 0), axis=1
+        )
         blocks = gathered.reshape(slices, -1, TILE)
         picked = jnp.take(blocks, cols_flat, axis=1).reshape(slices, tile_rows, kept, TILE)
         mixed = jnp.einsum("rkij,trkj->tri", tiles, picked, precision=lax.Precision.HIGHEST)

time: 225 us -> 253 us (1.12)
  waiting for transfers between devices: 160 us -> 96.2 us
  blocking collectives: 0 us -> 59.8 us
  local copies, waits for them, and re-layouts: 32.9 us -> 59.2 us
  starting transfers between devices: 7.67 us -> 26.3 us
  between operations: 14.1 us -> 1.02 us
    all_gather x3 -> x0, waiting for transfers between devices: 150 us -> none  [coulomb(): gathered = lax.all_gather(values, 'space', axis=1, tiled=True)]
    all_to_all x0 -> x1, blocking collectives: none -> 59.8 us  [coulomb(): lax.all_to_all(jnp.stack([values] * lax.axis_size('space')), 'space', 0, 0)]
    all_to_all x0 -> x2, waiting for transfers between devices: none -> 50.9 us  [coulomb(): lax.all_to_all(jnp.stack([values] * lax.axis_size('space')), 'space', 0, 0)]
    ppermute x1, waiting for transfers between devices: 0.01 us -> 37.5 us  [with_halo(): lax.ppermute(lax.slice_in_dim(block, block.shape[dim] - width, None, axis...]
    another operation x0 -> x9, local copies, waits for them, and re-layouts: none -> 24.9 us  [the longest x6 20.5 us: coulomb(): blocks = gathered.reshape(slices, -1, TILE)]
    all_to_all x0 -> x2, starting transfers between devices: none -> 17.9 us  [coulomb(): lax.all_to_all(jnp.stack([values] * lax.axis_size('space')), 'space', 0, 0)]
  transfers between devices with their start and end apart: 6 -> 5, of which waited for: 5 -> 4; matrix products, arithmetic and copies ran while one was open for 7% -> 6% of each run, Pallas kernels for 0% -> 0%
where the time goes in v1:
time: 253 us
  waiting for transfers between devices  96.2 us (38%)
  blocking collectives  59.8 us (24%)
  local copies, waits for them, and re-layouts  59.2 us (23%)
  starting transfers between devices  26.3 us (10%)
  matrix products  8.19 us (3%)
    all_to_all x1, blocking collectives, coulomb(): lax.all_to_all(jnp.stack([values] * lax.axis_size('space')), 'space', 0, 0)  59.8 us
    all_to_all x2, waiting for transfers between devices, coulomb(): lax.all_to_all(jnp.stack([values] * lax.axis_size('space')), 'space', 0, 0)  50.9 us
    ppermute x1, waiting for transfers between devices, with_halo(): lax.ppermute(lax.slice_in_dim(block, block.shape[dim] - width, None, axis...  37.5 us
    another operation x6, local copies, waits for them, and re-layouts, coulomb(): blocks = gathered.reshape(slices, -1, TILE)  20.5 us
    all_to_all x2, starting transfers between devices, coulomb(): lax.all_to_all(jnp.stack([values] * lax.axis_size('space')), 'space', 0, 0)  17.9 us
    gather x2, local copies, waits for them, and re-layouts, body(): jnp.take(widened, lookup.reshape(-1), axis=1)  13.8 us
    reshape x3, local copies, waits for them, and re-layouts, coulomb(): jnp.concatenate(lax.all_to_all(jnp.stack([values] * lax.axis_size('space'...  10.8 us
    dot_general x3, matrix products, coulomb(): jnp.einsum('rkij,trkj->tri', tiles, picked, precision=lax.Precision.HIGHEST)  8.19 us
  transfers between devices with their start and end apart: 5, of which 4 were waited for; matrix products, arithmetic and copies ran while one was open for 6% of the time, Pallas kernels for 0%

profile of v1, /device:TPU:1, one launch (start us, length us, event | category | flops | bytes accessed | tf_op | source)
XLA Modules:
  0.0 252.6 jit_solution(16299675782434079316)
XLA Ops:
  0.6 0.0 copy-start
  0.6 2.6 %stack.6 = f32[32,16,1024]{2,1,0:T(8,128)} broadcast(f32[16,1024]{1,0:T(8,128)} %param.8), dimensions={1,2} | broadcast | bytes 2162688 | tf_op jit(solution)/shard_map/stack | solution.py:42
  3.2 11.4 %all-to-all-start = ((f32[32,16,1024]{2,1,0:T(8,128)}), f32[32,16,1024]{2,1,0:T(8,128)}, u32[]{:S(2)}, u32[]{:S(2)}) async-start(f32[32,16,1024]{2,1,0:T(8,128)} %stack.6), calls=%async_computation | async-start | bytes 4194304 | tf_op jit(solution)/shard_map/all_to_all | solution.py:42
  14.6 0.1 reshape.95
  14.7 50.9 %all-to-all-done = f32[32,16,1024]{2,1,0:T(8,128)} async-done(((f32[32,16,1024]{2,1,0:T(8,128)}), f32[32,16,1024]{2,1,0:T(8,128)}, u32[]{:S(2)}, u32[]{:S(2)}) %all-to-all-start) | async-done | bytes 2097184 | tf_op jit(solution)/shard_map/all_to_all | solution.py:42
  65.7 4.1 %copy.23 = f32[16,32,1024]{2,1,0:T(8,128)} copy(f32[16,32,1024]{2,0,1:T(8,128)} %bitcast) | data formatting | bytes 4194304 | tf_op jit(solution)/shard_map/reshape | solution.py:41
  69.8 2.7 %reshape_reshape.9 = f32[16,256,128]{2,1,0:T(8,128)} reshape(f32[16,32,1024]{2,1,0:T(8,128)} %copy.23) | data formatting | bytes 4194304 | tf_op jit(solution)/shard_map/reshape;reshape | solution.py:44
  72.5 4.1 %copy.24 = f32[16,256,128]{2,0,1:T(8,128)} copy(f32[16,256,128]{2,1,0:T(8,128)} %reshape_reshape.9) | data formatting | bytes 4194304 | tf_op jit(solution)/shard_map/reshape;reshape | solution.py:44
  76.6 2.2 gather_fusion.1
  78.8 0.0 copy-start.8
  78.8 0.0 copy-start.15
  78.8 0.1 broadcast_select_fusion.2
  79.0 2.7 %fusion.5 = f32[8,2,8,128]{3,2,1,0:T(8,128)S(1)} fusion(f32[16,8,6,128]{3,0,2,1:T(8,128)S(1)} %bitcast.84, f32[8,6,128,128]{3,2,1,0:T(8,128)S(1)} %copy-done), kind=kOutput, calls=%fused_computation.12 | convolution fusion | flops 151011328 | bytes 3604480 | tf_op jit(solution)/shard_map/rkij,trkj->tri/dot_general | solution.py:46
  81.7 0.6 copy-done.1
  82.4 0.0 copy-start.11
  82.4 0.6 copy-done.11
  83.0 1.6 stack.7
  84.6 6.5 %all-to-all-start.1 = ((f32[32,16,1024]{2,1,0:T(8,128)}), f32[32,16,1024]{2,1,0:T(8,128)}, u32[]{:S(2)}, u32[]{:S(2)}) async-start(f32[32,16,1024]{2,1,0:T(8,128)} %stack.7), calls=%async_computation.1 | async-start | bytes 4194304 | tf_op jit(solution)/shard_map/all_to_all | solution.py:42
  91.1 4.4 %collective-permute-start = (f32[16,128]{1,0:T(8,128)S(1)}, f32[16,128]{1,0:T(8,128)S(1)}, u32[]{:S(2)}, u32[]{:S(2)}) collective-permute-start(f32[16,128]{1,0:T(8,128)S(1)} %get-tuple-element.8), channel_id=1, source_target_pairs={{0,16},{16,32},{32,48},{48,64},{64,80},{80,96},{96,112},{112,128},... | collective-permute-start | bytes 24584 | tf_op jit(solution)/shard_map/ppermute | solution.py:18
  95.5 1.9 collective-permute-start.1
  97.6 37.5 %collective-permute-done = f32[16,128]{1,0:T(8,128)S(1)} collective-permute-done((f32[16,128]{1,0:T(8,128)S(1)}, f32[16,128]{1,0:T(8,128)S(1)}, u32[]{:S(2)}, u32[]{:S(2)}) %collective-permute-start) | collective-permute-done | bytes 8224 | tf_op jit(solution)/shard_map/ppermute | solution.py:18
  135.1 3.4 %collective-permute-done.1 = f32[16,128]{1,0:T(8,128)S(1)} collective-permute-done((f32[16,128]{1,0:T(8,128)S(1)}, f32[16,128]{1,0:T(8,128)S(1)}, u32[]{:S(2)}, u32[]{:S(2)}) %collective-permute-start.1) | collective-permute-done | bytes 8224 | tf_op jit(solution)/shard_map/ppermute | solution.py:21
  138.5 1.1 copy.32
  139.6 12.0 %gather_fusion = f32[3072,16]{1,0:T(8,128)} fusion(f32[16,1280]{0,1:T(8,128)} %copy.32, s32[3072]{0:T(1024)S(1)} %broadcast_clamp_fusion), kind=kCustom, calls=%fused_computation.3 | custom fusion | bytes 405504 | tf_op jit(solution)/shard_map/jit(_take)/gather | solution.py:59
  151.6 1.8 copy.33
  153.5 0.6 copy-done.13
  154.1 2.1 collective-permute-start.2
  156.2 4.3 %collective-permute-done.2 = f32[1,1024]{1,0:T(1,128)S(1)} collective-permute-done((f32[1,1024]{1,0:T(1,128)S(1)}, f32[1,1024]{1,0:T(1,128)S(1)}, u32[]{:S(2)}, u32[]{:S(2)}) %collective-permute-start.2) | collective-permute-done | bytes 4128 | tf_op jit(solution)/shard_map/ppermute | solution.py:29
  160.6 4.1 %copy.26 = f32[16,32,1024]{2,1,0:T(8,128)} copy(f32[16,32,1024]{2,0,1:T(8,128)} %bitcast.6) | data formatting | bytes 4194304 | tf_op jit(solution)/shard_map/reshape | solution.py:41
  164.7 2.7 %reshape_reshape.10 = f32[16,256,128]{2,1,0:T(8,128)} reshape(f32[16,32,1024]{2,1,0:T(8,128)} %copy.26) | data formatting | bytes 4194304 | tf_op jit(solution)/shard_map/reshape;reshape | solution.py:44
  167.4 4.1 %copy.27 = f32[16,256,128]{2,0,1:T(8,128)} copy(f32[16,256,128]{2,1,0:T(8,128)} %reshape_reshape.10) | data formatting | bytes 4194304 | tf_op jit(solution)/shard_map/reshape;reshape | solution.py:44
  171.5 2.2 gather_fusion.2
  173.7 0.0 copy-start.5
  173.8 0.0 copy-start.14
  173.8 0.1 broadcast_select_fusion.1
  173.9 2.7 %fusion.3 = f32[8,2,8,128]{3,2,1,0:T(8,128)S(1)} fusion(f32[16,8,6,128]{3,0,2,1:T(8,128)S(1)} %bitcast.85, f32[8,6,128,128]{3,2,1,0:T(8,128)S(1)} %copy-done), kind=kOutput, calls=%fused_computation.9 | convolution fusion | flops 151011328 | bytes 3604480 | tf_op jit(solution)/shard_map/rkij,trkj->tri/dot_general | solution.py:46
  176.6 0.0 copy-done.2
  176.7 0.7 multiply_multiply_fusion
  177.4 0.2 stack.8
  177.6 59.8 %all_to_all.15 = f32[32,16,1024]{2,1,0:T(8,128)S(1)} all-to-all(f32[32,16,1024]{2,1,0:T(8,128)S(1)} %stack.8), channel_id=1, replica_groups=mesh['space'=32,'tm'=16] {'space'}, dimensions={0} | all-to-all | bytes 4194304 | tf_op jit(solution)/shard_map/all_to_all | solution.py:42
  237.5 2.5 copy.29
  240.0 2.7 %reshape_reshape.11 = f32[16,256,128]{2,1,0:T(8,128)} reshape(f32[16,32,1024]{2,1,0:T(8,128)} %copy.29) | data formatting | bytes 4194304 | tf_op jit(solution)/shard_map/reshape;reshape | solution.py:44
  242.7 4.1 %copy.30 = f32[16,256,128]{2,0,1:T(8,128)} copy(f32[16,256,128]{2,1,0:T(8,128)} %reshape_reshape.11) | data formatting | bytes 4194304 | tf_op jit(solution)/shard_map/reshape;reshape | solution.py:44
  246.9 2.2 gather_fusion.3
  249.1 0.1 broadcast_select_fusion
  249.2 2.7 %fusion.1 = f32[8,2,8,128]{3,2,1,0:T(8,128)S(1)} fusion(f32[16,8,6,128]{3,0,2,1:T(8,128)S(1)} %bitcast.83, f32[8,6,128,128]{3,2,1,0:T(8,128)S(1)} %copy-done), kind=kOutput, calls=%fused_computation.6 | convolution fusion | flops 151011328 | bytes 3604480 | tf_op jit(solution)/shard_map/rkij,trkj->tri/dot_general | solution.py:46
  251.9 0.0 copy-done.7
  251.9 0.6 bitcast_subtract_fusion
  (42 shorter events, 0.2 us)
Async XLA Ops:
  0.6 78.3 %copy-start = (f32[8,6,128,128]{3,2,1,0:T(8,128)S(1)}, f32[8,6,128,128]{3,2,1,0:T(8,128)}, u32[]{:S(2)}) copy-start(f32[8,6,128,128]{3,2,1,0:T(8,128)} %param.11) | copy-start | bytes 9437188
  3.2 11.4 %copy-start.18 = (s32[8,6]{1,0:T(8,128)S(1)}, s32[8,6]{1,0:T(8,128)}, u32[]{:S(2)}) copy-start(s32[8,6]{1,0:T(8,128)} %param.12) | copy-start | bytes 580
  3.2 62.5 %all-to-all-start = ((f32[32,16,1024]{2,1,0:T(8,128)}), f32[32,16,1024]{2,1,0:T(8,128)}, u32[]{:S(2)}, u32[]{:S(2)}) async-start(f32[32,16,1024]{2,1,0:T(8,128)} %stack.6), calls=%async_computation | async-start | bytes 4194304 | tf_op jit(solution)/shard_map/all_to_all | solution.py:42
  78.8 3.5 %copy-start.8 = (f32[16,1024]{1,0:T(8,128)S(1)}, f32[16,1024]{1,0:T(8,128)}, u32[]{:S(2)}) copy-start(f32[16,1024]{1,0:T(8,128)} %param.9) | copy-start | bytes 196612
  78.8 3.5 %copy-start.15 = (f32[16,1024]{1,0:T(8,128)S(1)}, f32[16,1024]{1,0:T(8,128)}, u32[]{:S(2)}) copy-start(f32[16,1024]{1,0:T(8,128)} %param.8) | copy-start | bytes 196612
  81.7 0.6 copy-start.1
  82.4 0.6 copy-start.11
  84.6 6.5 %copy-start.4 = (f32[16,1024]{1,0:T(8,128)S(1)}, f32[16,1024]{1,0:T(8,128)}, u32[]{:S(2)}) copy-start(f32[16,1024]{1,0:T(8,128)} %param.10) | copy-start | bytes 196612
  84.6 12.9 %copy-start.17 = (s32[3,1024]{1,0:T(4,128)S(1)}, s32[3,1024]{1,0:T(4,128)}, u32[]{:S(2)}) copy-start(s32[3,1024]{1,0:T(4,128)} %param.13) | copy-start | bytes 36868
  84.6 76.0 %all-to-all-start.1 = ((f32[32,16,1024]{2,1,0:T(8,128)}), f32[32,16,1024]{2,1,0:T(8,128)}, u32[]{:S(2)}, u32[]{:S(2)}) async-start(f32[32,16,1024]{2,1,0:T(8,128)} %stack.7), calls=%async_computation.1 | async-start | bytes 4194304 | tf_op jit(solution)/shard_map/all_to_all | solution.py:42
  91.1 44.0 %collective-permute-start = (f32[16,128]{1,0:T(8,128)S(1)}, f32[16,128]{1,0:T(8,128)S(1)}, u32[]{:S(2)}, u32[]{:S(2)}) collective-permute-start(f32[16,128]{1,0:T(8,128)S(1)} %get-tuple-element.8), channel_id=1, source_target_pairs={{0,16},{16,32},{32,48},{48,64},{64,80},{80,96},{96,112},{112,128},... | collective-permute-start | bytes 24584 | tf_op jit(solution)/shard_map/ppermute | solution.py:18
  95.5 42.9 %collective-permute-start.1 = (f32[16,128]{1,0:T(8,128)S(1)}, f32[16,128]{1,0:T(8,128)S(1)}, u32[]{:S(2)}, u32[]{:S(2)}) collective-permute-start(f32[16,128]{1,0:T(8,128)S(1)} %get-tuple-element.9), channel_id=1, source_target_pairs={{16,0},{32,16},{48,32},{64,48},{80,64},{96,80},{112,96},{128,112},... | collective-permute-start | bytes 24584 | tf_op jit(solution)/shard_map/ppermute | solution.py:21
  153.5 0.6 copy-start.13
  154.1 6.4 %collective-permute-start.2 = (f32[1,1024]{1,0:T(1,128)S(1)}, f32[1,1024]{1,0:T(1,128)S(1)}, u32[]{:S(2)}, u32[]{:S(2)}) collective-permute-start(f32[1,1024]{1,0:T(1,128)S(1)} %slice.39), channel_id=1, source_target_pairs={{0,1},{1,2},{2,3},{3,4},{4,5},{5,6},{6,7},{7,8},{8,9},{9,10},{10,1... | collective-permute-start | bytes 12296 | tf_op jit(solution)/shard_map/ppermute | solution.py:29
  173.7 2.9 %copy-start.2 = (f32[8,2,8,128]{3,2,1,0:T(8,128)S(1)}, f32[8,2,8,128]{3,2,1,0:T(8,128)}, u32[]{:S(2)}) copy-start(f32[8,2,8,128]{3,2,1,0:T(8,128)} %copy-done.1) | copy-start | bytes 196612
  173.7 2.9 %copy-start.5 = (f32[16,1024]{1,0:T(8,128)S(1)}, f32[16,1024]{1,0:T(8,128)}, u32[]{:S(2)}) copy-start(f32[16,1024]{1,0:T(8,128)} %param.10) | copy-start | bytes 196612
  173.7 2.9 %copy-start.9 = (f32[16,1024]{1,0:T(8,128)S(1)}, f32[16,1024]{1,0:T(8,128)}, u32[]{:S(2)}) copy-start(f32[16,1024]{1,0:T(8,128)} %param.9) | copy-start | bytes 196612
  173.8 2.9 %copy-start.12 = (f32[16,1024]{1,0:T(8,128)S(1)}, f32[16,1024]{1,0:T(8,128)}, u32[]{:S(2)}) copy-start(f32[16,1024]{1,0:T(8,128)} %copy-done.11) | copy-start | bytes 196612
  173.8 2.9 %copy-start.14 = (f32[16,1024]{1,0:T(8,128)S(1)}, f32[16,1024]{1,0:T(8,128)}, u32[]{:S(2)}) copy-start(f32[16,1024]{1,0:T(8,128)} %copy-done.13) | copy-start | bytes 196612
  176.6 60.8 %copy-start.6 = (f32[8,2,8,128]{3,2,1,0:T(8,128)}, f32[8,2,8,128]{3,2,1,0:T(8,128)S(1)}, u32[]{:S(2)}) copy-start(f32[8,2,8,128]{3,2,1,0:T(8,128)S(1)} %fusion.3) | copy-start | bytes 196612
  177.4 60.1 %copy-start.16 = (f32[16,1024]{1,0:T(8,128)}, f32[16,1024]{1,0:T(8,128)S(1)}, u32[]{:S(2)}) copy-start(f32[16,1024]{1,0:T(8,128)S(1)} %get-tuple-element.5) | copy-start | bytes 196612
  249.0 2.9 %copy-start.3 = (f32[8,2,8,128]{3,2,1,0:T(8,128)S(1)}, f32[8,2,8,128]{3,2,1,0:T(8,128)}, u32[]{:S(2)}) copy-start(f32[8,2,8,128]{3,2,1,0:T(8,128)} %copy-done.1) | copy-start | bytes 196612
  249.0 2.9 %copy-start.7 = (f32[8,2,8,128]{3,2,1,0:T(8,128)S(1)}, f32[8,2,8,128]{3,2,1,0:T(8,128)}, u32[]{:S(2)}) copy-start(f32[8,2,8,128]{3,2,1,0:T(8,128)} %copy-done.6) | copy-start | bytes 196612
  249.0 2.9 %copy-start.10 = (f32[16,1024]{1,0:T(8,128)S(1)}, f32[16,1024]{1,0:T(8,128)}, u32[]{:S(2)}) copy-start(f32[16,1024]{1,0:T(8,128)} %param.9) | copy-start | bytes 196612
